TPU v7x, 32 devices: a whole 2x2x4 slice. The times are simulated.
32 devices in a mesh: group: 4 (over y, x), dom: 8 (over z, core).
Axes of the slice: x: 2, y: 2, z: 4, core: 2. Of those that a mesh axis runs over, the one named last changes fastest.
Arguments:
- pin_feats: bfloat16 [32768, 256], P(('group', 'dom')), may hold values from -6 to 6
- w_self: bfloat16 [256, 256], replicated, may hold values from -0.375 to 0.375
- w_edge: bfloat16 [4, 256, 256], replicated, may hold values from -0.375 to 0.375
- w_head: bfloat16 [256, 1024], replicated, may hold values from -0.375 to 0.375
- w_out: bfloat16 [1024], replicated, may hold values from -0.1875 to 0.1875
- send_rows: int32 [32, 512], P(('group', 'dom')), may hold values from 0 to 1023
- edge_src: int32 [32, 4, 1024], P(('group', 'dom')), may hold values from 0 to 1535
- edge_dst: int32 [32, 4, 1024], P(('group', 'dom')), may hold values from 0 to 1023
- pin_owner: int32 [32768, 1], P(('group', 'dom')), may hold values from 0 to 31; in each aligned block of 1024 rows (0 to 1023, 1024 to 2047, ...) at most 64 rows name the same one
- pin_net: int32 [32768], P(('group', 'dom')), may hold values from 0 to 255
- net_target: float32 [8192], P(('group', 'dom')), may hold values from -6 to 6
Outputs:
- prediction: float32 [8192], P(('group', 'dom'))
- grad_feats: bfloat16 [32768, 256], P(('group', 'dom'))
- grad_self: float32 [256, 256], replicated
- grad_edge: float32 [4, 256, 256], replicated
- grad_head: float32 [256, 1024], replicated
- grad_out: float32 [1024], replicated
Inputs may be any that keep to these rules, and one draw needn't show every extreme that they name: `pin_owner`: among the pins of one device at most 64 name one owner, and in every draw some device sends exactly 64 pins to some owner.
All inputs are finite; a program needn't handle non-finite values.
Results may differ from a plain program's by a relative error of at most 0.0094.
Values may be sent and summed in bfloat16 or wider, within the bound.
No kernel may reach another device: no remote copies, remote signals or barrier semaphores. Data moves between devices by JAX's collectives and lax.ppermute only.
A program may use at most 64 MiB of HBM per device.

v0:
```python
import math
import jax
import jax.numpy as jnp
from jax import lax
from jax.sharding import PartitionSpec as P

F32 = jnp.float32
BF16 = jnp.bfloat16


def extended(block, sides, width):
    for axis, dim in sides:
        count = lax.axis_size(axis)
        forward = [(i, i + 1) for i in range(count - 1)]
        backward = [(target, source) for source, target in forward]
        low = lax.ppermute(
            lax.slice_in_dim(block, block.shape[dim] - width, None, axis=dim), axis, forward
        )
        high = lax.ppermute(lax.slice_in_dim(block, 0, width, axis=dim), axis, backward)
        block = jnp.concatenate([low, block, high], axis=dim)
    return block


def silu_slope(values):
    sigma_val = jax.nn.sigmoid(values)
    return sigma_val * (1.0 + values * (1.0 - sigma_val))


def one_hot(index, count):
    return (index[..., None] == jnp.arange(count, dtype=index.dtype)).astype(BF16)


def split_dot(spec, left, right):
    return jnp.einsum(
        spec, left, right.astype(F32), precision=lax.Precision.HIGHEST, preferred_element_type=F32
    )


def on_device(
    pin_feats,
    w_self,
    w_edge,
    w_head,
    w_out,
    send_rows,
    edge_src,
    edge_dst,
    pin_owner,
    pin_net,
    net_target,
):
    pin_count, feat_width = pin_feats.shape
    send_list = send_rows[0]
    halo_span = send_list.shape[0] // 2
    send_hot = one_hot(send_list, pin_count)
    outgoing = jnp.dot(send_hot, pin_feats, preferred_element_type=F32).astype(BF16)
    padded = extended(outgoing, (("dom", 0),), halo_span)
    node_table = jnp.concatenate([pin_feats, padded[:halo_span], padded[3 * halo_span :]], 0)
    table_rows = node_table.shape[0]
    sources = edge_src[0]
    endpoints = edge_dst[0]
    src_hot = one_hot(sources, table_rows)
    dst_hot = one_hot(endpoints, pin_count)
    gathered = jnp.einsum("ter,rd->ted", src_hot, node_table, preferred_element_type=F32).astype(
        BF16
    )
    edge_in = jnp.einsum("tep,ted->tpd", dst_hot, gathered, preferred_element_type=F32)
    summed = split_dot("tpk,tkd->pd", edge_in, w_edge)
    degree = jnp.sum(dst_hot.astype(F32), axis=(0, 1))
    inverse = 1.0 / (1.0 + degree)
    preact = jnp.dot(pin_feats, w_self, preferred_element_type=F32) + summed * inverse[:, None]
    hidden = jax.nn.silu(preact).astype(BF16)
    groups = lax.axis_size("group")
    domains = lax.axis_size("dom")
    owners = groups * domains
    capacity = max(2, 2 * pin_count // owners)
    net_count = net_target.shape[0]
    owner_ids = pin_owner[:, 0]
    owner_hot = one_hot(owner_ids, owners)
    earlier = (
        jnp.arange(pin_count, dtype=jnp.int32)[None, :]
        < jnp.arange(pin_count, dtype=jnp.int32)[:, None]
    ).astype(BF16)
    before = jnp.dot(earlier, owner_hot, preferred_element_type=F32)
    slot_rank = jnp.sum(before * owner_hot.astype(F32), axis=1).astype(jnp.int32)
    pin_slot = owner_ids * capacity + slot_rank
    slot_hot = one_hot(pin_slot, owners * capacity)
    net_code = (pin_net + 1).astype(BF16)[:, None]
    slot_nets = (
        jnp.dot(slot_hot.T, net_code, preferred_element_type=F32)[:, 0].astype(jnp.int32) - 1
    )
    slot_nets_in = lax.all_to_all(
        slot_nets.reshape(owners, capacity),
        ("group", "dom"),
        split_axis=0,
        concat_axis=0,
        tiled=True,
    ).reshape(-1)
    outbound = jnp.dot(slot_hot.T, hidden, preferred_element_type=F32).astype(BF16)
    inbound = lax.all_to_all(
        outbound.reshape(owners, capacity, feat_width),
        ("group", "dom"),
        split_axis=0,
        concat_axis=0,
        tiled=True,
    ).reshape(-1, feat_width)
    net_hot = one_hot(slot_nets_in, net_count)
    pooled = jnp.einsum("sn,sd->nd", net_hot, inbound, preferred_element_type=F32)
    pooled_b = pooled.astype(BF16)
    head_pre = jnp.dot(pooled_b, w_head, preferred_element_type=F32)
    activated = jax.nn.silu(head_pre).astype(BF16)
    predicted = jnp.dot(activated, w_out, preferred_element_type=F32)
    misfit = predicted - net_target
    head_grad = (misfit[:, None] * w_out.astype(F32)[None, :] * silu_slope(head_pre)).astype(BF16)
    head_sum = jnp.einsum("nd,nh->dh", pooled_b, head_grad, preferred_element_type=F32)
    out_sum = jnp.dot(misfit, activated.astype(F32), precision=lax.Precision.HIGHEST)
    head_totals = lax.psum(jnp.concatenate([head_sum, out_sum[None, :]], 0), ("group", "dom"))
    net_grad = jnp.einsum("nh,dh->nd", head_grad, w_head, preferred_element_type=F32).astype(BF16)
    returned = jnp.dot(net_hot, net_grad, preferred_element_type=F32).astype(BF16)
    arrived = lax.all_to_all(
        returned.reshape(owners, capacity, feat_width),
        ("group", "dom"),
        split_axis=0,
        concat_axis=0,
        tiled=True,
    ).reshape(-1, feat_width)
    pin_grad = jnp.dot(slot_hot, arrived, preferred_element_type=F32)
    preact_grad = (pin_grad * silu_slope(preact)).astype(BF16)
    self_sum = jnp.einsum("pk,pd->kd", pin_feats, preact_grad, preferred_element_type=F32)
    agg_grad = (preact_grad.astype(F32) * inverse[:, None]).astype(BF16)
    edge_rows = jnp.einsum("tep,pd->ted", dst_hot, agg_grad, preferred_element_type=F32).astype(
        BF16
    )
    edge_sum = jnp.einsum("tek,ted->tkd", gathered, edge_rows, preferred_element_type=F32)
    row_in = jnp.einsum("ter,ted->trd", src_hot, edge_rows, preferred_element_type=F32)
    table_grad = split_dot("trd,tkd->rk", row_in, w_edge)
    local_grad = (
        jnp.einsum("pd,kd->pk", preact_grad, w_self, preferred_element_type=F32)
        + table_grad[:pin_count]
    )
    halo_grad = table_grad[pin_count:].astype(BF16)
    back_padded = extended(halo_grad, (("dom", 0),), halo_span)
    received = jnp.concatenate([back_padded[:halo_span], back_padded[3 * halo_span :]], 0)
    grad_feats = (
        local_grad + jnp.einsum("sp,sd->pd", send_hot, received, preferred_element_type=F32)
    ).astype(BF16)
    self_sum, edge_sum, head_totals = lax.optimization_barrier((self_sum, edge_sum, head_totals))
    tail_totals = lax.psum((self_sum, edge_sum), ("group", "dom"))
    grad_scale = 1.0 / math.sqrt(pin_count * owners)
    return (
        predicted,
        grad_feats,
        tail_totals[0] * grad_scale,
        tail_totals[1] * grad_scale,
        head_totals[:feat_width] * grad_scale,
        head_totals[feat_width] * grad_scale,
    )


def solution(mesh):
    in_specs = (
        P(("group", "dom"), None),
        P(),
        P(),
        P(),
        P(),
        P(("group", "dom"), None),
        P(("group", "dom"), None, None),
        P(("group", "dom"), None, None),
        P(("group", "dom"), None),
        P(("group", "dom")),
        P(("group", "dom")),
    )
    out_specs = (P(("group", "dom")), P(("group", "dom"), None), P(), P(), P(), P())
    return jax.shard_map(
        on_device, mesh=mesh, in_specs=in_specs, out_specs=out_specs, check_vma=False
    )
```

profile of v0, /device:TPU:0, one launch (start us, length us, event | category | flops | bytes accessed | tf_op | source)
XLA Modules:
  0.0 383.9 jit_solution(4948331850442410509)
XLA Ops:
  7.2 0.0 copy-start
  7.2 0.7 add_convert_fusion
  7.9 1.3 fusion.31
  9.2 0.0 copy-start.2
  9.3 0.0 copy-start.14
  9.3 0.7 multiply_add_fusion
  10.0 1.5 fusion.11
  11.5 0.7 sub.16
  12.2 7.3 %all-to-all-start = ((s32[32,1,64]{2,1,0:T(1,128)}), s32[32,1,64]{2,1,0:T(1,128)S(1)}, u32[]{:S(2)}, u32[]{:S(2)}) async-start(s32[32,1,64]{2,1,0:T(1,128)} %sub.16), calls=%async_computation | async-start | bytes 32768 | tf_op jit(solution)/shard_map/all_to_all | solution.py:92
  19.5 0.5 fusion.28
  20.1 2.2 collective-permute-start
  22.2 1.3 collective-permute-start.1
  23.5 1.9 convert_reduce_fusion
  25.5 0.3 fusion.55
  25.8 0.0 collective-permute-done
  25.8 0.8 collective-permute-done.1
  26.6 4.8 %fusion.20 = bf16[4,1024,256]{2,1,0:T(8,128)(2,1)S(1)} fusion(s32[4,1024]{1,0:T(4,128)S(1)} %bitcast.74, bf16[256,256]{1,0:T(8,128)(2,1)S(1)} %collective-permute-done.1, bf16[256,256]{1,0:T(8,128)(2,1)S(1)} %collective-permute-done, bf16[1024,256]{1,0:T(8,128)(2,1)S(1)} %copy-done.2), kind=kOutput, calls=%fused_computation.29 | convolution fusion | flops 3230924800 | bytes 2899968 | tf_op jit(solution)/shard_map/ter,rd->ted/dot_general | solution.py:64
  31.5 0.0 copy-start.1
  31.5 5.8 %fusion.4 = f32[4,1024,256]{2,1,0:T(8,128)S(1)} fusion(bf16[4,1024,256]{2,1,0:T(8,128)(2,1)S(1)} %fusion.20, s32[4,1024]{1,0:T(4,128)S(1)} %bitcast.72), kind=kOutput, calls=%fused_computation.7 | convolution fusion | flops 2151677952 | bytes 6307840 | tf_op jit(solution)/shard_map/tep,ted->tpd/dot_general | solution.py:67
  37.2 2.1 fusion.24
  39.3 0.0 copy-start.7
  39.3 1.0 copy-done.7
  40.3 3.5 fusion.16
  43.8 0.0 all-to-all-done
  43.8 7.9 %all-to-all-start.1 = ((bf16[32,64,256]{2,1,0:T(8,128)(2,1)}), bf16[32,64,256]{2,1,0:T(8,128)(2,1)}, u32[]{:S(2)}, u32[]{:S(2)}) async-start(bf16[32,64,256]{2,1,0:T(8,128)(2,1)} %bitcast.60), calls=%async_computation.1 | async-start | bytes 2097152 | tf_op jit(solution)/shard_map/all_to_all | solution.py:100
  51.8 0.5 broadcast.42
  52.3 0.7 reduce.3
  53.0 0.1 eq.98
  53.0 26.2 %all-to-all-done.1 = bf16[32,64,256]{2,1,0:T(8,128)(2,1)} async-done(((bf16[32,64,256]{2,1,0:T(8,128)(2,1)}), bf16[32,64,256]{2,1,0:T(8,128)(2,1)}, u32[]{:S(2)}, u32[]{:S(2)}) %all-to-all-start.1) | async-done | bytes 1048608 | tf_op jit(solution)/shard_map/all_to_all | solution.py:100
  79.3 2.3 fusion.29
  81.6 0.0 copy-start.11
  81.6 0.4 multiply_convert_fusion.2
  82.1 0.8 copy-done.4
  82.8 0.2 fusion.56
  83.1 1.2 multiply_convert_fusion.1
  84.3 3.0 convolution_convert_fusion
  87.3 3.4 all-to-all-start.2
  90.7 0.0 all-reduce.4.cloned.1.call-start
  90.8 1.4 fusion.59
  92.1 1.4 fusion.58
  93.5 1.2 pad_maximum_fusion
  94.7 0.0 all-reduce.4.cloned.1.call-update
  94.7 0.0 all-reduce.6.cloned.1.call-start
  94.8 26.5 %all-to-all-done.2 = bf16[32,64,256]{2,1,0:T(8,128)(2,1)} async-done(((bf16[32,64,256]{2,1,0:T(8,128)(2,1)}), bf16[32,64,256]{2,1,0:T(8,128)(2,1)}, u32[]{:S(2)}, u32[]{:S(2)}) %all-to-all-start.2) | async-done | bytes 1048608 | tf_op jit(solution)/shard_map/all_to_all | solution.py:120
  121.2 3.3 fusion.26
  124.6 0.0 copy-start.5
  124.6 3.3 fusion.21
  127.9 0.0 copy-start.3
  127.9 9.3 %fusion = f32[4,1536,256]{2,1,0:T(8,128)} fusion(bf16[4,1024,256]{2,1,0:T(8,128)(2,1)S(1)} %fusion.21, s32[4,1024]{1,0:T(4,128)S(1)} %bitcast.75), kind=kOutput, calls=%fused_computation.1 | convolution fusion | flops 3227516928 | bytes 8404992 | tf_op jit(solution)/shard_map/ter,ted->trd/dot_general | solution.py:135
  137.2 1.0 convolution_bitcast_fusion.2
  138.3 1.9 fusion.57
  140.2 89.8 %all-reduce.4.cloned.1.call-done = f32[257,1024]{1,0:T(8,128)} async-done(((f32[257,1024]{1,0:T(8,128)}), f32[257,1024]{1,0:T(8,128)}) %all-reduce.4.cloned.1.call-update) | async-done | bytes 1052688 | tf_op jit(solution)/shard_map/psum | solution.py:117
  229.9 5.1 %fusion.54 = (bf16[1536,256]{1,0:T(8,128)(2,1)S(1)}, f32[1536,256]{1,0:T(8,128)S(1)}) fusion(f32[4,1536,256]{2,1,0:T(8,128)} %fusion, bf16[4,256,256]{2,1,0:T(8,128)(2,1)S(1)} %copy-done.1), kind=kOutput, calls=%fused_computation.83 | convolution fusion | flops 4832231424 | bytes 9175040 | tf_op jit(solution)/shard_map/trd,tkd->rk/dot_general | solution.py:34
  235.1 2.1 collective-permute-start.2
  237.2 1.3 collective-permute-start.3
  238.5 0.3 convolution_add_fusion
  238.8 0.0 all-reduce.6.cloned.1.call-update
  238.9 2.3 slice_multiply_fusion
  241.2 1.4 slice_multiply_fusion.1
  242.6 1.6 fusion.27
  244.2 128.8 %all-reduce.6.cloned.1.call-done = (f32[256,256]{0,1:T(8,128)}, f32[4,256,256]{2,1,0:T(8,128)}) async-done(((f32[256,256]{0,1:T(8,128)}, f32[4,256,256]{2,1,0:T(8,128)}), (f32[256,256]{0,1:T(8,128)}, f32[4,256,256]{2,1,0:T(8,128)})) %all-reduce.6.cloned.1.call-update) | async-done | bytes 1310736 | tf_op jit(solution)/shard_map/psum | solution.py:148
  373.0 1.0 broadcast_multiply_fusion.1
  373.9 0.8 copy.18
  374.8 2.3 broadcast_multiply_fusion
  (31 shorter events, 0.1 us)
Async XLA Ops:
  7.2 74.4 %copy-start = (bf16[256,1024]{1,0:T(8,128)(2,1)S(1)}, bf16[256,1024]{1,0:T(8,128)(2,1)}, u32[]{:S(2)}) copy-start(bf16[256,1024]{1,0:T(8,128)(2,1)} %param.14) | copy-start | bytes 1572868
  9.2 10.3 %copy-start.2 = (bf16[1024,256]{1,0:T(8,128)(2,1)S(1)}, bf16[1024,256]{1,0:T(8,128)(2,1)}, u32[]{:S(2)}) copy-start(bf16[1024,256]{1,0:T(8,128)(2,1)} %param.11) | copy-start | bytes 1572868
  9.3 10.3 %copy-start.14 = (s32[1,512]{1,0:T(1,128)S(1)}, s32[1,512]{1,0:T(1,128)}, u32[]{:S(2)}) copy-start(s32[1,512]{1,0:T(1,128)} %param.16) | copy-start | bytes 6148
  10.0 13.5 %copy-start.12 = (s32[1,4,1024]{2,1,0:T(4,128)S(1)}, s32[1,4,1024]{2,1,0:T(4,128)}, u32[]{:S(2)}) copy-start(s32[1,4,1024]{2,1,0:T(4,128)} %param.18) | copy-start | bytes 49156
  10.0 15.5 %copy-start.8 = (bf16[256,256]{1,0:T(8,128)(2,1)S(1)}, bf16[256,256]{1,0:T(8,128)(2,1)}, u32[]{:S(2)}) copy-start(bf16[256,256]{1,0:T(8,128)(2,1)} %param.12) | copy-start | bytes 393220
  11.5 15.1 %copy-start.13 = (s32[1,4,1024]{2,1,0:T(4,128)S(1)}, s32[1,4,1024]{2,1,0:T(4,128)}, u32[]{:S(2)}) copy-start(s32[1,4,1024]{2,1,0:T(4,128)} %param.17) | copy-start | bytes 49156
  12.2 31.6 %all-to-all-start = ((s32[32,1,64]{2,1,0:T(1,128)}), s32[32,1,64]{2,1,0:T(1,128)S(1)}, u32[]{:S(2)}, u32[]{:S(2)}) async-start(s32[32,1,64]{2,1,0:T(1,128)} %sub.16), calls=%async_computation | async-start | bytes 32768 | tf_op jit(solution)/shard_map/all_to_all | solution.py:92
  20.1 5.8 %collective-permute-start = (bf16[256,256]{1,0:T(8,128)(2,1)S(1)}, bf16[256,256]{1,0:T(8,128)(2,1)S(1)}, u32[]{:S(2)}, u32[]{:S(2)}) collective-permute-start(bf16[256,256]{1,0:T(8,128)(2,1)S(1)} %get-tuple-element.22), channel_id=1, source_target_pairs={{0,1},{1,2},{2,3},{3,4},{4,5},{5,6},{6,7},{8,9},{9,10},{10,11},{11... | collective-permute-start | bytes 393224 | tf_op jit(solution)/shard_map/ppermute | solution.py:16
  22.2 4.4 %collective-permute-start.1 = (bf16[256,256]{1,0:T(8,128)(2,1)S(1)}, bf16[256,256]{1,0:T(8,128)(2,1)S(1)}, u32[]{:S(2)}, u32[]{:S(2)}) collective-permute-start(bf16[256,256]{1,0:T(8,128)(2,1)S(1)} %get-tuple-element.23), channel_id=1, source_target_pairs={{1,0},{2,1},{3,2},{4,3},{5,4},{6,5},{7,6},{9,8},{10,9},{11,10},{12... | collective-permute-start | bytes 393224 | tf_op jit(solution)/shard_map/ppermute | solution.py:19
  31.5 5.8 %copy-start.1 = (bf16[4,256,256]{2,1,0:T(8,128)(2,1)S(1)}, bf16[4,256,256]{2,1,0:T(8,128)(2,1)}, u32[]{:S(2)}) copy-start(bf16[4,256,256]{2,1,0:T(8,128)(2,1)} %param.13) | copy-start | bytes 1572868
  39.3 1.0 copy-start.7
  43.8 7.9 %copy-start.9 = (bf16[1024]{0:T(1024)(128)(2,1)S(1)}, bf16[1024]{0:T(1024)(128)(2,1)}, u32[]{:S(2)}) copy-start(bf16[1024]{0:T(1024)(128)(2,1)} %param.15) | copy-start | bytes 6148
  43.8 35.5 %all-to-all-start.1 = ((bf16[32,64,256]{2,1,0:T(8,128)(2,1)}), bf16[32,64,256]{2,1,0:T(8,128)(2,1)}, u32[]{:S(2)}, u32[]{:S(2)}) async-start(bf16[32,64,256]{2,1,0:T(8,128)(2,1)} %bitcast.60), calls=%async_computation.1 | async-start | bytes 2097152 | tf_op jit(solution)/shard_map/all_to_all | solution.py:100
  81.6 1.5 copy-start.11
  82.0 0.8 copy-start.4
  83.1 4.2 %copy-start.10 = (f32[1,256]{1,0:T(1,128)}, f32[1,256]{1,0:T(1,128)S(1)}, u32[]{:S(2)}) copy-start(f32[1,256]{1,0:T(1,128)S(1)} %fusion.56) | copy-start | bytes 3076
  87.3 33.9 %all-to-all-start.2 = ((bf16[32,64,256]{2,1,0:T(8,128)(2,1)}), bf16[32,64,256]{2,1,0:T(8,128)(2,1)}, u32[]{:S(2)}, u32[]{:S(2)}) async-start(bf16[32,64,256]{2,1,0:T(8,128)(2,1)} %bitcast.59), calls=%async_computation.2 | async-start | bytes 2097152 | tf_op jit(solution)/shard_map/all_to_all | solution.py:120
  90.7 139.2 %all-reduce.4.cloned.1.call-start = ((), (), s32[]{:S(2)}) async-start(), calls=%async_computation.3 | async-start | bytes 2162688 | tf_op jit(solution)/shard_map/psum | solution.py:117
  94.7 278.2 %all-reduce.6.cloned.1.call-start = ((), (), s32[]{:S(2)}) async-start(), calls=%async_computation.4 | async-start | bytes 2621440 | tf_op jit(solution)/shard_map/psum | solution.py:148
  124.6 12.7 %copy-start.5 = (bf16[1024,256]{1,0:T(8,128)(2,1)}, bf16[1024,256]{1,0:T(8,128)(2,1)S(1)}, u32[]{:S(2)}) copy-start(bf16[1024,256]{1,0:T(8,128)(2,1)S(1)} %fusion.26) | copy-start | bytes 1572868
  127.9 9.4 %copy-start.3 = (bf16[1024,256]{1,0:T(8,128)(2,1)S(1)}, bf16[1024,256]{1,0:T(8,128)(2,1)}, u32[]{:S(2)}) copy-start(bf16[1024,256]{1,0:T(8,128)(2,1)} %param.11) | copy-start | bytes 1572868
  140.2 98.3 %copy-start.6 = (bf16[1024,256]{1,0:T(8,128)(2,1)S(1)}, bf16[1024,256]{1,0:T(8,128)(2,1)}, u32[]{:S(2)}) copy-start(bf16[1024,256]{1,0:T(8,128)(2,1)} %copy-done.5) | copy-start | bytes 1572868
  235.1 7.5 %collective-permute-start.2 = (bf16[256,256]{1,0:T(8,128)(2,1)S(1)}, bf16[256,256]{1,0:T(8,128)(2,1)S(1)}, u32[]{:S(2)}, u32[]{:S(2)}) collective-permute-start(bf16[256,256]{1,0:T(8,128)(2,1)S(1)} %get-tuple-element.20), channel_id=1, source_target_pairs={{0,1},{1,2},{2,3},{3,4},{4,5},{5,6},{6,7},{8,9},{9,10},{10,11},{11... | collective-permute-start | bytes 393224 | tf_op jit(solution)/shard_map/ppermute | solution.py:16
  237.2 5.4 %collective-permute-start.3 = (bf16[256,256]{1,0:T(8,128)(2,1)S(1)}, bf16[256,256]{1,0:T(8,128)(2,1)S(1)}, u32[]{:S(2)}, u32[]{:S(2)}) collective-permute-start(bf16[256,256]{1,0:T(8,128)(2,1)S(1)} %get-tuple-element.21), channel_id=1, source_target_pairs={{1,0},{2,1},{3,2},{4,3},{5,4},{6,5},{7,6},{9,8},{10,9},{11,10},{12... | collective-permute-start | bytes 393224 | tf_op jit(solution)/shard_map/ppermute | solution.py:19
Sparse Core Ops, SparseCore 0:
  97.0 132.9 all-reduce.3
  239.0 133.9 all-reduce.5
where the time goes:
time: 385 us; the launch traced here: 384 us
  waiting for transfers between devices  272 us (71%)
  matrix products  54.4 us (14%)
  starting transfers between devices  25.5 us (7%)
  between operations  14.4 us (4%)
  other arithmetic  13.6 us (4%)
  local copies, waits for them, and re-layouts  3.99 us (1%)
    psum x1, waiting for transfers between devices, on_device(): tail_totals = lax.psum((self_sum, edge_sum), ('group', 'dom'))  129 us
    psum x1, waiting for transfers between devices, on_device(): lax.psum(jnp.concatenate([head_sum, out_sum[None, :]], 0), ('group', 'dom'))  89.8 us
    all_to_all x1, waiting for transfers between devices, on_device(): lax.all_to_all(returned.reshape(owners, capacity, feat_width), ('group',...  26.5 us
    all_to_all x1, waiting for transfers between devices, on_device(): lax.all_to_all(outbound.reshape(owners, capacity, feat_width), ('group',...  26.2 us
    dot_general x1, matrix products, on_device(): jnp.einsum('ter,ted->trd', src_hot, edge_rows, preferred_element_type=F32)  9.33 us
    all_to_all x1, starting transfers between devices, on_device(): lax.all_to_all(outbound.reshape(owners, capacity, feat_width), ('group',...  7.91 us
  transfers between devices with their start and end apart: 9, of which 5 were waited for; matrix products, arithmetic and copies ran while one was open for 13% of the time, Pallas kernels for 0%

commit v1 on v0

--- a/solution.py
+++ b/solution.py
@@ -3,6 +3,7 @@
 import jax.numpy as jnp
 from jax import lax
 from jax.sharding import PartitionSpec as P
+from jax.lax import all_gather
 
 F32 = jnp.float32
 BF16 = jnp.bfloat16
@@ -114,7 +115,8 @@
     head_grad = (misfit[:, None] * w_out.astype(F32)[None, :] * silu_slope(head_pre)).astype(BF16)
     head_sum = jnp.einsum("nd,nh->dh", pooled_b, head_grad, preferred_element_type=F32)
     out_sum = jnp.dot(misfit, activated.astype(F32), precision=lax.Precision.HIGHEST)
-    head_totals = lax.psum(jnp.concatenate([head_sum, out_sum[None, :]], 0), ("group", "dom"))
+    here_x = jnp.concatenate([head_sum, out_sum[None, :]], 0)
+    head_totals = all_gather(here_x, ("group", "dom")).sum(axis=0)
     net_grad = jnp.einsum("nh,dh->nd", head_grad, w_head, preferred_element_type=F32).astype(BF16)
     returned = jnp.dot(net_hot, net_grad, preferred_element_type=F32).astype(BF16)
     arrived = lax.all_to_all(

time: 385 us -> 456 us (1.18)
  blocking collectives: 0 us -> 51.3 us
  waiting for transfers between devices: 272 us -> 292 us
  other arithmetic: 13.6 us -> 21.1 us
  matrix products: 54.4 us -> 49.6 us
    all_gather x0 -> x1, waiting for transfers between devices: none -> 139 us  [on_device(): head_totals = all_gather(here_x, ('group', 'dom')).sum(axis=0)]
    psum x1 -> x0, waiting for transfers between devices: 89.8 us -> none  [on_device(): lax.psum(jnp.concatenate([head_sum, out_sum[None, :]], 0), ('group', 'dom'))]
    all_to_all x0 -> x1, blocking collectives: none -> 51.3 us  [on_device(): lax.all_to_all(returned.reshape(owners, capacity, feat_width), ('group',...]
    all_to_all x1 -> x0, waiting for transfers between devices: 26.5 us -> none  [on_device(): lax.all_to_all(returned.reshape(owners, capacity, feat_width), ('group',...]
    reduce_sum x0 -> x1, other arithmetic: none -> 12 us  [on_device(): head_totals = all_gather(here_x, ('group', 'dom')).sum(axis=0)]
  transfers between devices with their start and end apart: 9 -> 8, of which waited for: 5 -> 3; matrix products, arithmetic and copies ran while one was open for 13% -> 14% of each run, Pallas kernels for 0% -> 0%
where the time goes in v1:
time: 456 us; the launch traced here: 455 us
  waiting for transfers between devices  292 us (64%)
  blocking collectives  51.3 us (11%)
  matrix products  49.6 us (11%)
  starting transfers between devices  22.2 us (5%)
  other arithmetic  21.1 us (5%)
  between operations  14.5 us (3%)
  local copies, waits for them, and re-layouts  4.65 us (1%)
    all_gather x1, waiting for transfers between devices, on_device(): head_totals = all_gather(here_x, ('group', 'dom')).sum(axis=0)  139 us
    psum x1, waiting for transfers between devices, on_device(): tail_totals = lax.psum((self_sum, edge_sum), ('group', 'dom'))  126 us
    all_to_all x1, blocking collectives, on_device(): lax.all_to_all(returned.reshape(owners, capacity, feat_width), ('group',...  51.3 us
    all_to_all x1, waiting for transfers between devices, on_device(): lax.all_to_all(outbound.reshape(owners, capacity, feat_width), ('group',...  26.2 us
    reduce_sum x1, other arithmetic, on_device(): head_totals = all_gather(here_x, ('group', 'dom')).sum(axis=0)  12 us
  transfers between devices with their start and end apart: 8, of which 3 were waited for; matrix products, arithmetic and copies ran while one was open for 14% of the time, Pallas kernels for 0%

profile of v1, /device:TPU:0, one launch (start us, length us, event | category | flops | bytes accessed | tf_op | source)
XLA Modules:
  0.0 455.4 jit_solution(11092118578520581222)
XLA Ops:
  7.2 0.0 copy-start
  7.2 1.6 fusion.28
  8.9 1.3 collective-permute-start.1
  10.2 3.0 collective-permute-start
  13.2 0.5 fusion.31
  13.8 0.0 copy-start.3
  13.8 0.0 copy-start.9
  13.8 0.0 copy-start.16
  13.8 0.0 copy-start.17
  13.9 1.5 fusion.11
  15.3 0.7 sub.16
  16.0 7.3 %all-to-all-start = ((s32[32,1,64]{2,1,0:T(1,128)}), s32[32,1,64]{2,1,0:T(1,128)S(1)}, u32[]{:S(2)}, u32[]{:S(2)}) async-start(s32[32,1,64]{2,1,0:T(1,128)} %sub.16), calls=%async_computation | async-start | bytes 32768 | tf_op jit(solution)/shard_map/all_to_all | solution.py:93
  23.4 0.3 fusion.55
  23.7 1.9 convert_reduce_fusion
  25.6 0.0 copy-start.15
  25.7 0.6 copy-done.15
  26.3 5.7 %fusion.20 = bf16[4,1024,256]{2,1,0:T(8,128)(2,1)S(1)} fusion(s32[4,1024]{1,0:T(4,128)S(1)} %bitcast.77, bf16[256,256]{1,0:T(8,128)(2,1)S(1)} %collective-permute-done.1, bf16[256,256]{1,0:T(8,128)(2,1)} %copy-done.15, bf16[1024,256]{1,0:T(8,128)(2,1)S(1)} %copy-done.3), kind=kOutput, calls=%fused_computation.29 | convolution fusion | flops 3230924800 | bytes 2899968 | tf_op jit(solution)/shard_map/ter,rd->ted/dot_general | solution.py:65
  32.1 0.0 copy-start.2
  32.1 5.8 %fusion.4 = f32[4,1024,256]{2,1,0:T(8,128)S(1)} fusion(bf16[4,1024,256]{2,1,0:T(8,128)(2,1)S(1)} %fusion.20, s32[4,1024]{1,0:T(4,128)S(1)} %bitcast.75), kind=kOutput, calls=%fused_computation.7 | convolution fusion | flops 2151677952 | bytes 6307840 | tf_op jit(solution)/shard_map/tep,ted->tpd/dot_general | solution.py:68
  37.8 2.1 fusion.24
  39.9 0.0 copy-start.7
  39.9 1.0 copy-done.7
  40.9 3.5 fusion.16
  44.4 0.0 all-to-all-done
  44.4 6.0 %all-to-all-start.1 = ((bf16[32,64,256]{2,1,0:T(8,128)(2,1)}), bf16[32,64,256]{2,1,0:T(8,128)(2,1)}, u32[]{:S(2)}, u32[]{:S(2)}) async-start(bf16[32,64,256]{2,1,0:T(8,128)(2,1)} %bitcast.61), calls=%async_computation.1 | async-start | bytes 2097152 | tf_op jit(solution)/shard_map/all_to_all | solution.py:101
  50.4 0.0 all-gather.4.cloned.1.call-start
  50.5 0.5 broadcast.42
  51.0 0.7 reduce.4
  51.7 0.1 eq.98
  51.8 26.2 %all-to-all-done.1 = bf16[32,64,256]{2,1,0:T(8,128)(2,1)} async-done(((bf16[32,64,256]{2,1,0:T(8,128)(2,1)}), bf16[32,64,256]{2,1,0:T(8,128)(2,1)}, u32[]{:S(2)}, u32[]{:S(2)}) %all-to-all-start.1) | async-done | bytes 1048608 | tf_op jit(solution)/shard_map/all_to_all | solution.py:101
  78.0 2.3 fusion.29
  80.2 0.0 copy-start.14
  80.3 0.5 multiply_convert_fusion.2
  80.7 0.2 fusion.56
  81.0 0.3 fusion.59
  81.3 0.4 multiply_convert_fusion.1
  81.7 0.0 copy-start.5
  81.7 0.8 copy-done.5
  82.5 0.3 fusion.58
  82.8 1.1 maximum_bitcast_fusion
  83.9 0.0 all-gather.4.cloned.1.call-update
  84.0 0.0 all-reduce.3.cloned.1.call-start
  84.0 3.0 convolution_convert_fusion
  87.0 51.3 %all_to_all.16 = bf16[32,64,256]{2,1,0:T(8,128)(2,1)S(1)} all-to-all(bf16[32,64,256]{2,1,0:T(8,128)(2,1)} %bitcast.63), channel_id=1, replica_groups=mesh['group'=4,'dom'=8] {'group','dom'}, dimensions={0} | all-to-all | bytes 2097152 | tf_op jit(solution)/shard_map/all_to_all | solution.py:122
  138.3 1.8 fusion.26
  140.1 3.3 fusion.21
  143.4 8.0 %fusion = f32[4,1536,256]{2,1,0:T(8,128)S(1)} fusion(bf16[4,1024,256]{2,1,0:T(8,128)(2,1)S(1)} %fusion.21, s32[4,1024]{1,0:T(4,128)S(1)} %bitcast.78), kind=kOutput, calls=%fused_computation.1 | convolution fusion | flops 3227516928 | bytes 8404992 | tf_op jit(solution)/shard_map/ter,ted->trd/dot_general | solution.py:137
  151.3 3.1 fusion.54
  154.5 1.3 collective-permute-start.3
  155.8 3.3 collective-permute-start.2
  159.1 1.3 convolution_add_fusion
  160.4 1.9 fusion.57
  162.3 1.0 convolution_bitcast_fusion.2
  163.3 139.3 %all-gather.4.cloned.1.call-done = f32[32,257,1024]{2,1,0:T(8,128)} async-done(((f32[1,257,1024]{2,1,0:T(8,128)}), f32[32,257,1024]{2,1,0:T(8,128)}) %all-gather.4.cloned.1.call-update) | async-done | bytes 33685520 | tf_op jit(solution)/shard_map/all_gather | solution.py:119
  302.6 12.0 %reduce_sum.29 = f32[257,1024]{1,0:T(8,128)S(1)} reduce(f32[32,257,1024]{2,1,0:T(8,128)} %all-gather.4.cloned.1.call-done, f32[]{:T(128)} %constant.7.clone.1), dimensions={0}, to_apply=%region_2.3 | reduce | flops 8158208 | bytes 34738180 | tf_op jit(solution)/shard_map/reduce_sum | solution.py:119
  314.6 0.0 all-reduce.3.cloned.1.call-update
  314.6 0.0 collective-permute-done.3
  314.7 1.6 fusion.27
  316.3 0.6 slice_multiply_fusion.1
  316.9 1.1 slice_multiply_fusion
  318.0 126.5 %all-reduce.3.cloned.1.call-done = (f32[256,256]{0,1:T(8,128)}, f32[4,256,256]{2,1,0:T(8,128)}) async-done(((f32[256,256]{0,1:T(8,128)}, f32[4,256,256]{2,1,0:T(8,128)}), (f32[256,256]{0,1:T(8,128)}, f32[4,256,256]{2,1,0:T(8,128)})) %all-reduce.3.cloned.1.call-update) | async-done | bytes 1310736 | tf_op jit(solution)/shard_map/psum | solution.py:150
  444.4 1.0 broadcast_multiply_fusion.1
  445.4 0.8 copy.20
  446.3 2.3 broadcast_multiply_fusion
  (39 shorter events, 0.2 us)
Async XLA Ops:
  7.2 73.1 %copy-start = (bf16[256,1024]{1,0:T(8,128)(2,1)S(1)}, bf16[256,1024]{1,0:T(8,128)(2,1)}, u32[]{:S(2)}) copy-start(bf16[256,1024]{1,0:T(8,128)(2,1)} %param.14) | copy-start | bytes 1572868
  7.2 6.0 %copy-start.12 = (s32[1024,1]{0,1:T(1,128)S(1)}, s32[1024,1]{0,1:T(1,128)}, u32[]{:S(2)}) copy-start(s32[1024,1]{0,1:T(1,128)} %param.19) | copy-start | bytes 12292
  7.2 6.6 %copy-start.13 = (s32[1024]{0:T(1024)S(1)}, s32[1024]{0:T(1024)}, u32[]{:S(2)}) copy-start(s32[1024]{0:T(1024)} %param.20) | copy-start | bytes 12292
  8.9 16.8 %collective-permute-start.1 = (bf16[256,256]{1,0:T(8,128)(2,1)S(1)}, bf16[256,256]{1,0:T(8,128)(2,1)S(1)}, u32[]{:S(2)}, u32[]{:S(2)}) collective-permute-start(bf16[256,256]{1,0:T(8,128)(2,1)S(1)} %get-tuple-element.29), channel_id=1, source_target_pairs={{1,0},{2,1},{3,2},{4,3},{5,4},{6,5},{7,6},{9,8},{10,9},{11,10},{12... | collective-permute-start | bytes 393224 | tf_op jit(solution)/shard_map/ppermute | solution.py:20
  10.2 15.5 %collective-permute-start = (bf16[256,256]{1,0:T(8,128)(2,1)S(1)}, bf16[256,256]{1,0:T(8,128)(2,1)S(1)}, u32[]{:S(2)}, u32[]{:S(2)}) collective-permute-start(bf16[256,256]{1,0:T(8,128)(2,1)S(1)} %get-tuple-element.28), channel_id=1, source_target_pairs={{0,1},{1,2},{2,3},{3,4},{4,5},{5,6},{6,7},{8,9},{9,10},{10,11},{11... | collective-permute-start | bytes 393224 | tf_op jit(solution)/shard_map/ppermute | solution.py:17
  13.8 9.6 %copy-start.3 = (bf16[1024,256]{1,0:T(8,128)(2,1)S(1)}, bf16[1024,256]{1,0:T(8,128)(2,1)}, u32[]{:S(2)}) copy-start(bf16[1024,256]{1,0:T(8,128)(2,1)} %param.11) | copy-start | bytes 1572868
  13.8 9.6 %copy-start.9 = (bf16[256,256]{1,0:T(8,128)(2,1)S(1)}, bf16[256,256]{1,0:T(8,128)(2,1)}, u32[]{:S(2)}) copy-start(bf16[256,256]{1,0:T(8,128)(2,1)} %param.12) | copy-start | bytes 393220
  13.8 9.8 %copy-start.16 = (s32[1,4,1024]{2,1,0:T(4,128)S(1)}, s32[1,4,1024]{2,1,0:T(4,128)}, u32[]{:S(2)}) copy-start(s32[1,4,1024]{2,1,0:T(4,128)} %param.18) | copy-start | bytes 49156
  13.8 12.5 %copy-start.17 = (s32[1,4,1024]{2,1,0:T(4,128)S(1)}, s32[1,4,1024]{2,1,0:T(4,128)}, u32[]{:S(2)}) copy-start(s32[1,4,1024]{2,1,0:T(4,128)} %param.17) | copy-start | bytes 49156
  16.0 28.4 %all-to-all-start = ((s32[32,1,64]{2,1,0:T(1,128)}), s32[32,1,64]{2,1,0:T(1,128)S(1)}, u32[]{:S(2)}, u32[]{:S(2)}) async-start(s32[32,1,64]{2,1,0:T(1,128)} %sub.16), calls=%async_computation | async-start | bytes 32768 | tf_op jit(solution)/shard_map/all_to_all | solution.py:93
  25.6 0.7 copy-start.15
  32.1 5.8 %copy-start.2 = (bf16[4,256,256]{2,1,0:T(8,128)(2,1)S(1)}, bf16[4,256,256]{2,1,0:T(8,128)(2,1)}, u32[]{:S(2)}) copy-start(bf16[4,256,256]{2,1,0:T(8,128)(2,1)} %param.13) | copy-start | bytes 1572868
  39.9 1.0 copy-start.7
  44.4 6.0 %copy-start.10 = (bf16[1024]{0:T(1024)(128)(2,1)S(1)}, bf16[1024]{0:T(1024)(128)(2,1)}, u32[]{:S(2)}) copy-start(bf16[1024]{0:T(1024)(128)(2,1)} %param.15) | copy-start | bytes 6148
  44.4 33.5 %all-to-all-start.1 = ((bf16[32,64,256]{2,1,0:T(8,128)(2,1)}), bf16[32,64,256]{2,1,0:T(8,128)(2,1)}, u32[]{:S(2)}, u32[]{:S(2)}) async-start(bf16[32,64,256]{2,1,0:T(8,128)(2,1)} %bitcast.61), calls=%async_computation.1 | async-start | bytes 2097152 | tf_op jit(solution)/shard_map/all_to_all | solution.py:101
  50.4 252.2 %all-gather.4.cloned.1.call-start = ((), (), s32[]{:S(2)}) async-start(), calls=%async_computation.3 | async-start | bytes 35684352 | tf_op jit(solution)/shard_map/all_gather | solution.py:119
  80.2 0.7 copy-start.14
  80.9 3.0 copy-start.11
  81.7 0.8 copy-start.5
  84.0 360.5 %all-reduce.3.cloned.1.call-start = ((), (), s32[]{:S(2)}) async-start(), calls=%async_computation.4 | async-start | bytes 2621440 | tf_op jit(solution)/shard_map/psum | solution.py:150
  87.0 51.3 %copy-start.8 = (f32[1024,256]{1,0:T(8,128)S(1)}, f32[1024,256]{1,0:T(8,128)}, u32[]{:S(2)}) copy-start(f32[1024,256]{1,0:T(8,128)} %copy-done.7) | copy-start | bytes 3145732
  154.5 160.1 %collective-permute-start.3 = (bf16[256,256]{1,0:T(8,128)(2,1)S(1)}, bf16[256,256]{1,0:T(8,128)(2,1)S(1)}, u32[]{:S(2)}, u32[]{:S(2)}) collective-permute-start(bf16[256,256]{1,0:T(8,128)(2,1)S(1)} %get-tuple-element.27), channel_id=1, source_target_pairs={{1,0},{2,1},{3,2},{4,3},{5,4},{6,5},{7,6},{9,8},{10,9},{11,10},{12... | collective-permute-start | bytes 393224 | tf_op jit(solution)/shard_map/ppermute | solution.py:20
  155.8 158.9 %collective-permute-start.2 = (bf16[256,256]{1,0:T(8,128)(2,1)S(1)}, bf16[256,256]{1,0:T(8,128)(2,1)S(1)}, u32[]{:S(2)}, u32[]{:S(2)}) collective-permute-start(bf16[256,256]{1,0:T(8,128)(2,1)S(1)} %get-tuple-element.26), channel_id=1, source_target_pairs={{0,1},{1,2},{2,3},{3,4},{4,5},{5,6},{6,7},{8,9},{9,10},{10,11},{11... | collective-permute-start | bytes 393224 | tf_op jit(solution)/shard_map/ppermute | solution.py:17
  160.4 1.9 copy-start.4
  163.3 151.4 %copy-start.6 = (f32[1024,256]{1,0:T(8,128)S(1)}, f32[1024,256]{1,0:T(8,128)}, u32[]{:S(2)}) copy-start(f32[1024,256]{1,0:T(8,128)} %convolution_add_fusion) | copy-start | bytes 3145732
  163.3 151.4 %copy-start.18 = (s32[1,512]{1,0:T(1,128)S(1)}, s32[1,512]{1,0:T(1,128)}, u32[]{:S(2)}) copy-start(s32[1,512]{1,0:T(1,128)} %param.16) | copy-start | bytes 6148
  316.9 131.7 %copy-start.1 = (bf16[256,1024]{1,0:T(8,128)(2,1)S(1)}, bf16[256,1024]{1,0:T(8,128)(2,1)}, u32[]{:S(2)}) copy-start(bf16[256,1024]{1,0:T(8,128)(2,1)} %param.14) | copy-start | bytes 1572868
Sparse Core Ops, SparseCore 0:
  84.1 218.5 all-gather.3
  314.7 129.6 all-reduce.2
